TPU v7x, 512 devices: a whole 4x8x8 slice. The times are simulated.
512 devices in a mesh: seq: 64 (over z, x, core), head: 8 (over y).
Axes of the slice: x: 4, y: 8, z: 8, core: 2. Of those that a mesh axis runs over, the one named last changes fastest.
Arguments:
- projected: float32 [65536, 2560], P(('seq', 'head')), may hold values from -6 to 6
- out_grads: float32 [65536, 2048], P(('seq', 'head')), may hold values from -6 to 6
- conv_weight: float32 [3, 2560], replicated, may hold values from -2.4 to 2.4
- doc_lengths: int32 [16], replicated, may hold values from 1 to 32768, 65536 in all
Outputs:
- grad_projected: float32 [65536, 2560], P(('seq', 'head'))
- grad_conv: float32 [3, 2560], replicated
Inputs may be any that keep to these rules, and one draw needn't show every extreme that they name: `doc_lengths`: the 16 documents fill the 65536 tokens end to end; the longest holds exactly half of 65536 tokens.
All inputs are finite; a program needn't handle non-finite values.
Results may differ from a plain program's by a relative error of at most 0.0003.
Values sent between devices are 32-bit elements; how exact they have to be, the bound alone decides.
No kernel may reach another device: no remote copies, remote signals or barrier semaphores. Data moves between devices by JAX's collectives and lax.ppermute only.
A program may use at most 128 MiB of HBM per device.

v0:
```python
import math
import jax
import jax.numpy as jnp
import numpy as np
from jax import lax
from jax.sharding import PartitionSpec as P

KEY_DIM = 16
HEAD_DIM = 128
HIGHEST = lax.Precision.HIGHEST


def carried_in(x, axis, combine, identity, reverse):
    length, here = (lax.axis_size(axis), lax.axis_index(axis))
    everything = jax.tree.map(lambda part: lax.all_gather(part, axis), x)
    start = jax.tree.map(
        lambda part, zero: jnp.broadcast_to(jnp.asarray(zero, part.dtype), part.shape), x, identity
    )

    def lap(k, before):
        at = length - 1 - k if reverse else k
        reached = at > here if reverse else at < here
        new = combine(before, jax.tree.map(lambda part: part[at], everything))
        return jax.tree.map(lambda a, b: jnp.where(reached, a, b), new, before)

    return lax.fori_loop(0, length, lap, start)


def passed_along(value, axis, steps):
    count = lax.axis_size(axis)
    initial, last = (max(0, -steps), min(count, count - steps))
    return lax.ppermute(value, axis, [(source, source + steps) for source in range(initial, last)])


def feature_map(columns):
    key_size = columns.shape[1]
    upper_i, upper_j = np.triu_indices(key_size)
    factors = np.where(upper_i == upper_j, 1.0 / math.sqrt(2.0), 1.0).astype(np.float32)
    products = columns[:, upper_i, :] * columns[:, upper_j, :] * jnp.asarray(factors)[None, :, None]
    constant = jnp.ones((columns.shape[0], 1, columns.shape[2]), jnp.float32)
    return jnp.concatenate([constant, columns, products], axis=1)


def doc_place(doc_lengths, anchor, amount):
    positions = anchor + jnp.arange(amount, dtype=jnp.int32)
    starts = jnp.cumsum(doc_lengths) - doc_lengths
    begins = jnp.max(jnp.where(starts[None, :] <= positions[:, None], starts[None, :], 0), axis=1)
    return (begins, positions - begins)


def conv_forward(signal, leading, weights, offsets):
    row_count = signal.shape[0]
    behind = jnp.concatenate([leading, signal], axis=0)
    back_one = behind[1 : row_count + 1] * (offsets[0:row_count] >= 1).astype(jnp.float32)[:, None]
    back_two = behind[0:row_count] * (offsets[0:row_count] >= 2).astype(jnp.float32)[:, None]
    return weights[0] * signal + weights[1] * back_one + weights[2] * back_two


def conv_backward(grad_rows, trailing, signal, leading, weights, offsets):
    row_count = grad_rows.shape[0]
    ahead_rows = jnp.concatenate([grad_rows, trailing], axis=0)
    ahead_one = (
        ahead_rows[1 : row_count + 1]
        * (offsets[1 : row_count + 1] >= 1).astype(jnp.float32)[:, None]
    )
    ahead_two = (
        ahead_rows[2 : row_count + 2]
        * (offsets[2 : row_count + 2] >= 2).astype(jnp.float32)[:, None]
    )
    grad_signal = weights[0] * grad_rows + weights[1] * ahead_one + weights[2] * ahead_two
    behind = jnp.concatenate([leading, signal], axis=0)
    own_one = (offsets[0:row_count] >= 1).astype(jnp.float32)[:, None]
    own_two = (offsets[0:row_count] >= 2).astype(jnp.float32)[:, None]
    grad_weights = jnp.stack(
        [
            jnp.sum(grad_rows * signal, axis=0),
            jnp.sum(grad_rows * behind[1 : row_count + 1] * own_one, axis=0),
            jnp.sum(grad_rows * behind[0:row_count] * own_two, axis=0),
        ],
        axis=0,
    )
    return (grad_signal, grad_weights)


def combine(earlier, following):
    carry_keep = 1.0 - following[2]
    return (
        following[0] + carry_keep[:, None, None] * earlier[0],
        following[1] + carry_keep[:, None] * earlier[1],
        jnp.maximum(earlier[2], following[2]),
    )


def attention_grads(mixed_rows, out_flat, begins, stretch_start):
    length = mixed_rows.shape[0]
    head_width = 2 * KEY_DIM + HEAD_DIM
    local_heads = mixed_rows.shape[1] // head_width
    block_len = min(128, length)
    blocks = length // block_len
    scale_key = KEY_DIM ** (-0.25)
    shaped = mixed_rows.reshape(length, local_heads, head_width)
    query_cols = jnp.transpose(shaped[:, :, :KEY_DIM], (1, 2, 0)) * scale_key
    key_cols = jnp.transpose(shaped[:, :, KEY_DIM : 2 * KEY_DIM], (1, 2, 0)) * scale_key
    values = shaped[:, :, 2 * KEY_DIM :]
    upstream = out_flat.reshape(length, local_heads, HEAD_DIM)
    query_feat, query_pull = jax.vjp(feature_map, query_cols)
    key_feat, key_pull = jax.vjp(feature_map, key_cols)
    feat_count = query_feat.shape[1]
    last_begin = begins[length - 1]
    has_start = (last_begin >= stretch_start).astype(jnp.float32).reshape(1)
    tail_mask = (begins == last_begin).astype(jnp.float32)
    tail_feat = key_feat * tail_mask[None, None, :]
    tail_state = jnp.einsum("hfl,lhe->hfe", tail_feat, values, precision=HIGHEST)
    tail_norm = jnp.sum(tail_feat, axis=2)
    identity = (jnp.zeros_like(tail_state), jnp.zeros_like(tail_norm), jnp.zeros((1,), jnp.float32))
    prefix = carried_in((tail_state, tail_norm, has_start), "seq", combine, identity, False)
    causal = jnp.arange(block_len)[:, None] >= jnp.arange(block_len)[None, :]
    indices = jnp.arange(blocks, dtype=jnp.int32)

    def forward_block(carried, block_index):
        carry_state, carry_norm = carried
        offset_rows = block_index * block_len
        block_start = stretch_start + offset_rows
        query_blk = lax.dynamic_slice_in_dim(query_feat, offset_rows, block_len, 2)
        key_blk = lax.dynamic_slice_in_dim(key_feat, offset_rows, block_len, 2)
        value_blk = lax.dynamic_slice_in_dim(values, offset_rows, block_len, 0)
        doc_blk = lax.dynamic_slice_in_dim(begins, offset_rows, block_len, 0)
        allowed = causal & (doc_blk[:, None] == doc_blk[None, :])
        scores = jnp.where(
            allowed[None], jnp.einsum("hft,hfs->hts", query_blk, key_blk, precision=HIGHEST), 0.0
        )
        from_carry = (doc_blk < block_start).astype(jnp.float32)
        numerator = jnp.einsum("hts,she->the", scores, value_blk, precision=HIGHEST) + from_carry[
            :, None, None
        ] * jnp.einsum("hft,hfe->the", query_blk, carry_state, precision=HIGHEST)
        denominator = jnp.sum(scores, axis=2) + from_carry[None, :] * jnp.einsum(
            "hft,hf->ht", query_blk, carry_norm, precision=HIGHEST
        )
        block_tail = (doc_blk == doc_blk[block_len - 1]).astype(jnp.float32)
        carry_keep = (doc_blk[block_len - 1] < block_start).astype(jnp.float32)
        tail_keys = key_blk * block_tail[None, None, :]
        next_state = (
            jnp.einsum("hfs,she->hfe", tail_keys, value_blk, precision=HIGHEST)
            + carry_keep * carry_state
        )
        next_norm = jnp.sum(tail_keys, axis=2) + carry_keep * carry_norm
        return ((next_state, next_norm), (numerator, denominator, carry_state, carry_norm, scores))

    forward_out = lax.scan(forward_block, (prefix[0], prefix[1]), indices)
    numerators, denominators, states, norms, kept_scores = forward_out[1]
    denom_rows = jnp.transpose(denominators, (0, 2, 1)).reshape(length, local_heads)
    attended = numerators.reshape(length, local_heads, HEAD_DIM) / denom_rows[:, :, None]
    grad_num = upstream / denom_rows[:, :, None]
    scalar_grad = -jnp.sum(upstream * attended, axis=2) / denom_rows
    lead_mask = (begins < stretch_start).astype(jnp.float32)
    lead_feat = query_feat * lead_mask[None, None, :]
    lead_state = jnp.einsum("hfl,lhe->hfe", lead_feat, grad_num, precision=HIGHEST)
    lead_norm = jnp.einsum("hfl,lh->hf", lead_feat, scalar_grad, precision=HIGHEST)
    suffix = carried_in((lead_state, lead_norm, has_start), "seq", combine, identity, True)

    def backward_block(carried, inputs):
        back_state, back_norm = carried
        block_index, carry_state, carry_norm, scores = inputs
        offset_rows = block_index * block_len
        block_start = stretch_start + offset_rows
        query_blk = lax.dynamic_slice_in_dim(query_feat, offset_rows, block_len, 2)
        key_blk = lax.dynamic_slice_in_dim(key_feat, offset_rows, block_len, 2)
        value_blk = lax.dynamic_slice_in_dim(values, offset_rows, block_len, 0)
        doc_blk = lax.dynamic_slice_in_dim(begins, offset_rows, block_len, 0)
        grad_blk = lax.dynamic_slice_in_dim(grad_num, offset_rows, block_len, 0)
        scalar_blk = lax.dynamic_slice_in_dim(scalar_grad, offset_rows, block_len, 0)
        scalar_cols = scalar_blk.T
        allowed = causal & (doc_blk[:, None] == doc_blk[None, :])
        dscores = jnp.where(
            allowed[None],
            jnp.einsum("the,she->hts", grad_blk, value_blk, precision=HIGHEST)
            + scalar_cols[:, :, None],
            0.0,
        )
        from_carry = (doc_blk < block_start).astype(jnp.float32)
        block_tail = (doc_blk == doc_blk[block_len - 1]).astype(jnp.float32)
        carry_keep = (doc_blk[block_len - 1] < block_start).astype(jnp.float32)
        grad_query = jnp.einsum("hts,hfs->hft", dscores, key_blk, precision=HIGHEST) + from_carry[
            None, None, :
        ] * (
            jnp.einsum("hfe,the->hft", carry_state, grad_blk, precision=HIGHEST)
            + carry_norm[:, :, None] * scalar_cols[:, None, :]
        )
        grad_key = jnp.einsum("hts,hft->hfs", dscores, query_blk, precision=HIGHEST) + block_tail[
            None, None, :
        ] * (
            jnp.einsum("hfe,she->hfs", back_state, value_blk, precision=HIGHEST)
            + back_norm[:, :, None]
        )
        grad_value = jnp.einsum("hts,the->she", scores, grad_blk, precision=HIGHEST) + block_tail[
            :, None, None
        ] * jnp.einsum("hfs,hfe->she", key_blk, back_state, precision=HIGHEST)
        lead_blk = query_blk * from_carry[None, None, :]
        next_state = (
            jnp.einsum("hft,the->hfe", lead_blk, grad_blk, precision=HIGHEST)
            + carry_keep * back_state
        )
        next_norm = (
            jnp.einsum("hft,th->hf", lead_blk, scalar_blk, precision=HIGHEST)
            + carry_keep * back_norm
        )
        return ((next_state, next_norm), (grad_query, grad_key, grad_value))

    swept_back = lax.scan(
        backward_block, (suffix[0], suffix[1]), (indices, states, norms, kept_scores), reverse=True
    )
    grad_qblocks, grad_kblocks, grad_vblocks = swept_back[1]
    query_grad = jnp.transpose(grad_qblocks, (1, 2, 0, 3)).reshape(local_heads, feat_count, length)
    key_grad = jnp.transpose(grad_kblocks, (1, 2, 0, 3)).reshape(local_heads, feat_count, length)
    value_grad = grad_vblocks.reshape(length, local_heads, HEAD_DIM)
    query_in = jnp.transpose(query_pull(query_grad)[0] * scale_key, (2, 0, 1))
    key_in = jnp.transpose(key_pull(key_grad)[0] * scale_key, (2, 0, 1))
    return jnp.concatenate([query_in, key_in, value_grad], axis=2).reshape(
        length, local_heads * head_width
    )


def on_device(projected, out_grads, conv_weight, doc_lengths):
    row_count = projected.shape[0]
    head_count = lax.axis_size("head")
    seq_index = lax.axis_index("seq")
    head_index = lax.axis_index("head")
    group_len = row_count * head_count
    token_base = (seq_index * head_count + head_index) * row_count
    stretch_start = seq_index * group_len
    token_begins, token_offsets = doc_place(doc_lengths, token_base, row_count + 2)
    leading = passed_along(projected[row_count - 2 :], ("seq", "head"), 1)
    outgoing = conv_forward(projected, leading, conv_weight, token_offsets)
    arrived, upstream = (
        lax.all_to_all(outgoing, "head", split_axis=1, concat_axis=0, tiled=True),
        lax.all_to_all(out_grads, "head", split_axis=1, concat_axis=0, tiled=True),
    )
    group_begins, group_offsets = doc_place(doc_lengths, stretch_start, group_len + 2)
    grad_mixed = attention_grads(arrived, upstream, group_begins[:group_len], stretch_start)
    returned = lax.all_to_all(grad_mixed, "head", split_axis=0, concat_axis=1, tiled=True)
    trailing = passed_along(returned[:2], ("seq", "head"), -1)
    grad_projected, weight_part = conv_backward(
        returned, trailing, projected, leading, conv_weight, token_offsets
    )
    grad_conv = lax.psum(weight_part, ("seq", "head"))
    return (grad_projected, grad_conv)


def solution(mesh):
    return jax.shard_map(
        on_device,
        mesh=mesh,
        in_specs=(P(("seq", "head"), None), P(("seq", "head"), None), P(), P()),
        out_specs=(P(("seq", "head"), None), P()),
        check_vma=False,
    )
```

profile of v0, /device:TPU:1, one launch (start us, length us, event | category | flops | bytes accessed | tf_op | source)
XLA Modules:
  0.0 1203.6 jit_solution(1783652886522364890)
XLA Ops:
  8.1 4.0 collective-permute-start
  17.7 3.1 multiply_add_fusion.1
  20.8 6.1 all-to-all-start
  28.4 33.2 %all-to-all-done = f32[128,8,320]{0,2,1:T(8,128)S(1)} async-done(((f32[128,8,320]{0,2,1:T(8,128)}), f32[128,8,320]{0,2,1:T(8,128)S(1)}, u32[]{:S(2)}, u32[]{:S(2)}) %all-to-all-start) | async-done | bytes 1310752 | tf_op jit(solution)/shard_map/all_to_all | solution.py:235
  64.6 3.1 gather_fusion.1
  67.7 3.0 gather_fusion.2
  70.7 3.0 gather_fusion.3
  73.7 3.1 fusion.91
  76.8 4.8 broadcast_multiply_fusion.1
  81.6 2.3 fusion.81
  85.3 3.6 all-to-all-start.1
  91.7 131.3 %all-reduce = f32[64]{0:T(128)S(1)} all-reduce(f32[64]{0:T(128)S(1)} %dynamic-update-slice), channel_id=1, replica_groups=mesh['seq'=64,'head'=8] {'seq'}, use_global_device_ids=true, to_apply=%add | all-reduce | flops 64 | bytes 512
  224.6 2.4 reshape.170
  230.0 2.5 copy.167
  232.5 51.4 %all-gather.4 = f32[64,2,153]{2,1,0:T(2,128)S(1)} all-gather(f32[1,2,153]{2,1,0:T(2,128)S(1)} %copy.127), channel_id=3, replica_groups=mesh['seq'=64,'head'=8] {'seq'}, dimensions={0}, use_global_device_ids=true | all-gather | bytes 79560 | tf_op jit(solution)/shard_map/all_gather | solution.py:15
  283.9 187.7 %while.82 = (s32[]{:T(128)}, f32[2,153,128]{2,1,0:T(8,128)S(1)}, f32[2,153]{1,0:T(2,128)S(1)}, s32[]{:T(128)}, f32[64,2,153,128]{3,2,1,0:T(8,128)}, /*index=5*/f...) while((s32[]{:T(128)}, f32[2,153,128]{2,1,0:T(8,128)S(1)}, ...), condition=%wide.region_5.6_spmd.clone, body=%wide.region_4.5_spmd.clone.sunk | while | flops 157901 | bytes 473831 | solution.py:26
  472.9 110.3 %while.80 = (s32[]{:T(128)}, f32[2,153,128]{2,1,0:T(8,128)S(1)}, f32[2,153]{1,0:T(2,128)S(1)}, f32[8,128,2,128]{1,0,3,2:T(8,128)}, f32[8,2,128]{2,1,0:T(2,128)S(...) while((s32[]{:T(128)}, f32[2,153,128]{2,1,0:T(8,128)S(1)}, ...), condition=%wide.region_9.10_spmd.clone, body=%wide.region_6.9_spmd.clone.sunk | while | flops 231664960 | bytes 3280461 | solution.py:149
  476.9 4.8 dynamic_update_slice.74
  490.7 4.8 dynamic_update_slice.74
  504.5 4.8 dynamic_update_slice.74
  518.3 4.8 dynamic_update_slice.74
  532.1 4.8 dynamic_update_slice.74
  545.9 4.8 dynamic_update_slice.74
  559.7 4.8 dynamic_update_slice.74
  573.4 4.8 dynamic_update_slice.74
  583.1 2.4 reshape.171
  588.4 2.3 fusion.85
  590.7 2.8 fusion.83
  593.5 49.5 %all-gather.5 = f32[64,2,153]{2,1,0:T(2,128)S(1)} all-gather(f32[1,2,153]{2,1,0:T(2,128)S(1)} %bitcast.282), channel_id=5, replica_groups=mesh['seq'=64,'head'=8] {'seq'}, dimensions={0}, use_global_device_ids=true | all-gather | bytes 79560 | tf_op jit(solution)/shard_map/all_gather | solution.py:15
  643.0 36.5 %all-gather.11.cloned.1.call-done = f32[128,153,128]{2,1,0:T(8,128)} async-done(((f32[2,153,128]{2,1,0:T(8,128)}), f32[128,153,128]{2,1,0:T(8,128)}) %all-gather.11.cloned.1.call-update) | async-done | bytes 10027024 | tf_op jit(solution)/shard_map/all_gather | solution.py:15
  679.5 195.2 %while.83 = (s32[]{:T(128)}, f32[2,153,128]{2,1,0:T(8,128)S(1)}, f32[2,153]{1,0:T(2,128)S(1)}, s32[]{:T(128)}, f32[64,2,153,128]{3,2,1,0:T(8,128)}, /*index=5*/f...) while((s32[]{:T(128)}, f32[2,153,128]{2,1,0:T(8,128)S(1)}, ...), condition=%wide.region_12.13_spmd.clone, body=%wide.region_11.12_spmd.clone.sunk | while | flops 157905 | bytes 473893 | solution.py:26
  878.2 112.1 %while.81 = (s32[]{:T(128)}, f32[2,153,128]{2,1,0:T(8,128)S(1)}, f32[2,153]{1,0:T(2,128)S(1)}, f32[8,2,153,128]{3,2,1,0:T(8,128)}, f32[8,2,153,128]{3,2,1,0:T(8,...) while((s32[]{:T(128)}, f32[2,153,128]{2,1,0:T(8,128)S(1)}, ...), condition=%wide.region_14.15_spmd.clone, body=%wide.region_13.14_spmd.clone.sunk | while | flops 462717824 | bytes 4866477 | solution.py:209
  913.1 2.0 fusion.196
  927.1 2.0 fusion.196
  941.1 2.0 fusion.196
  955.1 2.0 fusion.196
  983.2 2.0 fusion.196
  990.4 2.0 copy.137
  998.9 5.9 fusion.90
  1004.9 14.0 %scatter_fusion = f32[2,16,1024]{2,0,1:T(2,128)S(1)} fusion(f32[2,16,1024]{2,0,1:T(2,128)S(1)} %split.16, s32[136]{0:T(256)S(1)} %copy-done.23, f32[136,2,1024]{2,1,0:T(2,128)} %get-tuple-element.1103), kind=kCustom, calls=%fused_computation.4 | custom fusion | flops 278528 | bytes 3342880 | tf_op jit(solution)/shard_map/transpose(jvp())/scatter-add | solution.py:39
  1018.9 7.6 scatter_fusion.1
  1027.7 7.6 scatter_fusion.3
  1035.3 7.6 scatter_fusion.2
  1044.3 2.7 pad_maximum_fusion
  1048.3 40.7 %all_to_all.51 = f32[8,128,320]{1,2,0:T(8,128)S(1)} all-to-all(f32[8,128,320]{1,2,0:T(8,128)S(1)} %copy.143), channel_id=1, replica_groups=mesh['seq'=64,'head'=8] {'head'}, dimensions={0} | all-to-all | bytes 2621440 | tf_op jit(solution)/shard_map/all_to_all | solution.py:240
  1089.1 2.2 multiply_reduce_fusion.2
  1093.7 95.5 %psum.7 = f32[3,2560]{1,0:T(4,128)} all-reduce(f32[3,2560]{1,0:T(4,128)S(1)} %pad_maximum_fusion.5), channel_id=1, replica_groups=mesh['seq'=64,'head'=8] {'seq','head'}, use_global_device_ids=true, to_apply=%region_22.23 | all-reduce | flops 7680 | bytes 61440 | tf_op jit(solution)/shard_map/psum | solution.py:245
  1190.7 4.4 fusion.77
  (814 shorter events, 574.3 us)
Async XLA Ops:
  8.1 9.1 collective-permute-start
  14.4 3.2 copy-start.25
  14.4 3.2 copy-start.27
  15.4 2.2 copy-start.16
  15.4 2.2 copy-start.18
  15.4 2.2 copy-start.20
  17.2 3.6 copy-start.3
  17.6 3.1 copy-start.5
  20.8 6.9 copy-start.24
  20.8 6.9 copy-start.23
  20.8 40.9 %all-to-all-start = ((f32[128,8,320]{0,2,1:T(8,128)}), f32[128,8,320]{0,2,1:T(8,128)S(1)}, u32[]{:S(2)}, u32[]{:S(2)}) async-start(f32[128,8,320]{0,2,1:T(8,128)} %bitcast.265), calls=%async_computation | async-start | bytes 2621440 | tf_op jit(solution)/shard_map/all_to_all | solution.py:235
  26.9 257.1 %all-gather.9.cloned.1.call-start = ((), (), s32[]{:S(2)}) async-start(), calls=%async_computation.3 | async-start | bytes 10649600 | tf_op jit(solution)/shard_map/all_gather | solution.py:15
  27.0 62.6 %copy-start.22 = (s32[1026]{0:T(1024)}, s32[1026]{0:T(1024)S(1)}, u32[]{:S(2)}) copy-start(s32[1026]{0:T(1024)S(1)} %select_reduce_fusion) | copy-start | bytes 12316
  64.6 9.1 copy-start.7
  70.7 3.0 copy-start.29
  81.6 2.3 copy-start.15
  85.3 137.7 %all-to-all-start.1 = ((f32[128,8,256]{0,2,1:T(8,128)}), f32[128,8,256]{0,2,1:T(8,128)S(1)}, u32[]{:S(2)}, u32[]{:S(2)}) async-start(f32[128,8,256]{0,2,1:T(8,128)} %bitcast.273), calls=%async_computation.1 | async-start | bytes 2097152 | tf_op jit(solution)/shard_map/all_to_all | solution.py:236
  88.8 590.7 %all-gather.11.cloned.1.call-start = ((), (), s32[]{:S(2)}) async-start(), calls=%async_computation.4 | async-start | bytes 10649600 | tf_op jit(solution)/shard_map/all_gather | solution.py:15
  227.0 1.7 copy-start.11
  228.1 1.4 copy-start.10
  471.6 1.2 slice-start.1
  585.5 2.9 copy-start.2
  587.4 1.0 copy-start
  992.4 1.7 copy-start.9
  995.9 3.1 copy-start.8
  997.8 7.0 copy-start.1
  1004.9 14.0 %copy-start.14 = (f32[136,2,1024]{2,1,0:T(2,128)S(1)}, f32[136,2,1024]{2,1,0:T(2,128)}, u32[]{:S(2)}) copy-start(f32[136,2,1024]{2,1,0:T(2,128)} %get-tuple-element.1102) | copy-start | bytes 3342340
  1026.5 1.2 copy-start.13
  1027.7 7.6 slice-start
  1027.7 7.6 copy-start.12
  1048.0 41.0 %copy-start.26 = (f32[128]{0:T(128)S(1)}, f32[128]{0:T(128)}, u32[]{:S(2)}) copy-start(f32[128]{0:T(128)} %copy-done.25) | copy-start | bytes 1540
  1048.1 41.0 %copy-start.28 = (f32[128]{0:T(128)S(1)}, f32[128]{0:T(128)}, u32[]{:S(2)}) copy-start(f32[128]{0:T(128)} %copy-done.27) | copy-start | bytes 1540
  1048.3 40.7 %copy-start.4 = (f32[128,2560]{0,1:T(8,128)S(1)}, f32[128,2560]{0,1:T(8,128)}, u32[]{:S(2)}) copy-start(f32[128,2560]{0,1:T(8,128)} %copy-done.3) | copy-start | bytes 3932164
  1048.3 40.7 %copy-start.6 = (f32[2,2560]{0,1:T(8,128)S(1)}, f32[2,2560]{0,1:T(8,128)}, u32[]{:S(2)}) copy-start(f32[2,2560]{0,1:T(8,128)} %copy-done.5) | copy-start | bytes 61444
  1091.3 99.4 %copy-start.17 = (f32[2560]{0:T(1024)S(1)}, f32[2560]{0:T(1024)}, u32[]{:S(2)}) copy-start(f32[2560]{0:T(1024)} %copy-done.16) | copy-start | bytes 30724
  1091.3 99.4 %copy-start.19 = (f32[2560]{0:T(1024)S(1)}, f32[2560]{0:T(1024)}, u32[]{:S(2)}) copy-start(f32[2560]{0:T(1024)} %copy-done.18) | copy-start | bytes 30724
  1091.3 99.4 %copy-start.21 = (f32[2560]{0:T(1024)S(1)}, f32[2560]{0:T(1024)}, u32[]{:S(2)}) copy-start(f32[2560]{0:T(1024)} %copy-done.20) | copy-start | bytes 30724
  1091.3 99.4 %copy-start.30 = (f32[128]{0:T(128)S(1)}, f32[128]{0:T(128)}, u32[]{:S(2)}) copy-start(f32[128]{0:T(128)} %get-tuple-element.1110) | copy-start | bytes 1540
  1091.3 99.4 %copy-start.31 = (f32[128]{0:T(128)S(1)}, f32[128]{0:T(128)}, u32[]{:S(2)}) copy-start(f32[128]{0:T(128)} %get-tuple-element.1112) | copy-start | bytes 1540
  1091.7 97.5 %collective-permute-start.1 = (f32[2,2560]{1,0:T(2,128)S(1)}, f32[2,2560]{1,0:T(2,128)S(1)}, u32[]{:S(2)}, u32[]{:S(2)}) collective-permute-start(f32[2,2560]{1,0:T(2,128)S(1)} %copy.144), channel_id=1, source_target_pairs={{1,0},{2,1},{3,2},{4,3},{5,4},{6,5},{7,6},{8,7},{9,8},{10,9},{11,1... | collective-permute-start | bytes 61448 | tf_op jit(solution)/shard_map/ppermute | solution.py:32
Sparse Core Ops, SparseCore 0:
  84.0 91.8 all-gather.8
  590.8 88.6 all-gather.10
where the time goes:
time: 1220 us; the launch traced here: 1200 us
  other arithmetic  462 us (38%)
  blocking collectives  368 us (30%)
  local copies, waits for them, and re-layouts  129 us (11%)
  matrix products  118 us (10%)
  waiting for transfers between devices  69.8 us (6%)
  loops' own time  25.3 us (2%)
  starting transfers between devices  15.7 us (1%)
  between operations  15.7 us (1%)
    select_n x256, other arithmetic, lap(): return jax.tree.map(lambda a, b: jnp.where(reached, a, b), new, before)  301 us
    unnamed x1, blocking collectives  131 us
    all_gather x2, blocking collectives, carried_in(): everything = jax.tree.map(lambda part: lax.all_gather(part, axis), x)  101 us
    psum x1, blocking collectives, on_device(): grad_conv = lax.psum(weight_part, ('seq', 'head'))  95.5 us
    sub x128, other arithmetic, combine(): carry_keep = 1.0 - following[2]  78.9 us
    dynamic_update_slice x48, local copies, waits for them, and re-layouts, attention_grads(): forward_out = lax.scan(forward_block, (prefix[0], prefix[1]), indices)  55 us
    all_to_all x1, blocking collectives, on_device(): lax.all_to_all(grad_mixed, 'head', split_axis=0, concat_axis=1, tiled=True)  40.7 us
    all_gather x2, waiting for transfers between devices, carried_in(): everything = jax.tree.map(lambda part: lax.all_gather(part, axis), x)  36.5 us
  transfers between devices with their start and end apart: 6, of which 2 were waited for; matrix products, arithmetic and copies ran while one was open for 2% of the time, Pallas kernels for 0%

commit v1 on v0

--- a/solution.py
+++ b/solution.py
@@ -242,7 +242,9 @@
     grad_projected, weight_part = conv_backward(
         returned, trailing, projected, leading, conv_weight, token_offsets
     )
-    grad_conv = lax.psum(weight_part, ("seq", "head"))
+    grad_conv = weight_part
+    for no in ("head", "seq"):
+        grad_conv = lax.psum(grad_conv, no)
     return (grad_projected, grad_conv)
 
 

time: 1220 us -> 1390 us (1.14)
  blocking collectives: 368 us -> 544 us
    psum x1 -> x2, blocking collectives: 95.5 us -> 271 us  [on_device(): grad_conv = lax.psum(grad_conv, no)]
  transfers between devices with their start and end apart: 6 -> 6, of which waited for: 2 -> 2; matrix products, arithmetic and copies ran while one was open for 2% -> 1% of each run, Pallas kernels for 0% -> 0%
where the time goes in v1:
time: 1390 us; the launch traced here: 1380 us
  blocking collectives  544 us (39%)
  other arithmetic  451 us (32%)
  local copies, waits for them, and re-layouts  135 us (10%)
  matrix products  118 us (8%)
  waiting for transfers between devices  69.8 us (5%)
  loops' own time  25.9 us (2%)
  starting transfers between devices  15.7 us (1%)
  between operations  15.6 us (1%)
    select_n x256, other arithmetic, lap(): return jax.tree.map(lambda a, b: jnp.where(reached, a, b), new, before)  294 us
    psum x2, blocking collectives, on_device(): grad_conv = lax.psum(grad_conv, no)  271 us
    unnamed x1, blocking collectives  132 us
    all_gather x2, blocking collectives, carried_in(): everything = jax.tree.map(lambda part: lax.all_gather(part, axis), x)  101 us
    sub x128, other arithmetic, combine(): carry_keep = 1.0 - following[2]  75.4 us
    dynamic_update_slice x48, local copies, waits for them, and re-layouts, attention_grads(): forward_out = lax.scan(forward_block, (prefix[0], prefix[1]), indices)  54.8 us
    all_to_all x1, blocking collectives, on_device(): lax.all_to_all(grad_mixed, 'head', split_axis=0, concat_axis=1, tiled=True)  40.8 us
    all_gather x2, waiting for transfers between devices, carried_in(): everything = jax.tree.map(lambda part: lax.all_gather(part, axis), x)  36.4 us
  transfers between devices with their start and end apart: 6, of which 2 were waited for; matrix products, arithmetic and copies ran while one was open for 1% of the time, Pallas kernels for 0%

profile of v1, /device:TPU:1, one launch (start us, length us, event | category | flops | bytes accessed | tf_op | source)
XLA Modules:
  0.0 1375.4 jit_solution(9665241873513913439)
XLA Ops:
  8.1 4.0 collective-permute-start
  17.0 3.1 multiply_add_fusion.1
  20.1 6.1 all-to-all-start
  27.7 33.3 %all-to-all-done = f32[128,8,320]{0,2,1:T(8,128)S(1)} async-done(((f32[128,8,320]{0,2,1:T(8,128)}), f32[128,8,320]{0,2,1:T(8,128)S(1)}, u32[]{:S(2)}, u32[]{:S(2)}) %all-to-all-start) | async-done | bytes 1310752 | tf_op jit(solution)/shard_map/all_to_all | solution.py:235
  64.8 3.0 gather_fusion
  67.8 3.1 gather_fusion.1
  70.9 3.0 gather_fusion.2
  73.9 3.1 gather_fusion.3
  77.0 3.4 fusion.91
  80.5 4.3 broadcast_multiply_fusion.1
  84.7 2.3 fusion.81
  88.4 3.6 all-to-all-start.1
  94.8 131.7 %all-reduce = f32[64]{0:T(128)S(1)} all-reduce(f32[64]{0:T(128)S(1)} %dynamic-update-slice), channel_id=1, replica_groups=mesh['seq'=64,'head'=8] {'seq'}, use_global_device_ids=true, to_apply=%add | all-reduce | flops 64 | bytes 512
  228.1 2.4 reshape.170
  233.5 2.5 copy.167
  236.0 51.6 %all-gather.4 = f32[64,2,153]{2,1,0:T(2,128)S(1)} all-gather(f32[1,2,153]{2,1,0:T(2,128)S(1)} %copy.127), channel_id=3, replica_groups=mesh['seq'=64,'head'=8] {'seq'}, dimensions={0}, use_global_device_ids=true | all-gather | bytes 79560 | tf_op jit(solution)/shard_map/all_gather | solution.py:15
  287.6 187.7 %while.82 = (s32[]{:T(128)}, f32[2,153,128]{2,1,0:T(8,128)S(1)}, f32[2,153]{1,0:T(2,128)S(1)}, s32[]{:T(128)}, f32[64,2,153,128]{3,2,1,0:T(8,128)}, /*index=5*/f...) while((s32[]{:T(128)}, f32[2,153,128]{2,1,0:T(8,128)S(1)}, ...), condition=%wide.region_5.6_spmd.clone, body=%wide.region_4.5_spmd.clone.sunk | while | flops 157901 | bytes 473831 | solution.py:26
  476.6 110.1 %while.80 = (s32[]{:T(128)}, f32[2,153,128]{2,1,0:T(8,128)S(1)}, f32[2,153]{1,0:T(2,128)S(1)}, f32[8,128,2,128]{1,0,3,2:T(8,128)}, f32[8,2,128]{2,1,0:T(2,128)S(...) while((s32[]{:T(128)}, f32[2,153,128]{2,1,0:T(8,128)S(1)}, ...), condition=%wide.region_9.10_spmd.clone, body=%wide.region_6.9_spmd.clone.sunk | while | flops 231664960 | bytes 3280461 | solution.py:149
  480.6 4.7 dynamic_update_slice.74
  494.4 4.7 dynamic_update_slice.74
  508.2 4.7 dynamic_update_slice.74
  521.9 4.7 dynamic_update_slice.74
  535.7 4.7 dynamic_update_slice.74
  549.5 4.7 dynamic_update_slice.74
  563.2 4.7 dynamic_update_slice.74
  577.0 4.7 dynamic_update_slice.74
  586.6 2.4 reshape.171
  591.9 2.3 fusion.85
  594.3 2.8 fusion.83
  597.0 49.5 %all-gather.5 = f32[64,2,153]{2,1,0:T(2,128)S(1)} all-gather(f32[1,2,153]{2,1,0:T(2,128)S(1)} %bitcast.282), channel_id=5, replica_groups=mesh['seq'=64,'head'=8] {'seq'}, dimensions={0}, use_global_device_ids=true | all-gather | bytes 79560 | tf_op jit(solution)/shard_map/all_gather | solution.py:15
  646.5 36.4 %all-gather.11.cloned.1.call-done = f32[128,153,128]{2,1,0:T(8,128)} async-done(((f32[2,153,128]{2,1,0:T(8,128)}), f32[128,153,128]{2,1,0:T(8,128)}) %all-gather.11.cloned.1.call-update) | async-done | bytes 10027024 | tf_op jit(solution)/shard_map/all_gather | solution.py:15
  683.0 184.7 %while.83 = (s32[]{:T(128)}, f32[2,153,128]{2,1,0:T(8,128)S(1)}, f32[2,153]{1,0:T(2,128)S(1)}, s32[]{:T(128)}, f32[64,2,153,128]{3,2,1,0:T(8,128)}, /*index=5*/f...) while((s32[]{:T(128)}, f32[2,153,128]{2,1,0:T(8,128)S(1)}, ...), condition=%wide.region_12.13_spmd.clone, body=%wide.region_11.12_spmd.clone.sunk | while | flops 157905 | bytes 473893 | solution.py:26
  871.2 113.0 %while.81 = (s32[]{:T(128)}, f32[2,153,128]{2,1,0:T(8,128)S(1)}, f32[2,153]{1,0:T(2,128)S(1)}, f32[8,2,153,128]{3,2,1,0:T(8,128)}, f32[8,2,153,128]{3,2,1,0:T(8,...) while((s32[]{:T(128)}, f32[2,153,128]{2,1,0:T(8,128)S(1)}, ...), condition=%wide.region_14.15_spmd.clone, body=%wide.region_13.14_spmd.clone.sunk | while | flops 462717824 | bytes 4866477 | solution.py:209
  906.4 2.0 fusion.196
  948.7 2.0 fusion.196
  962.8 2.0 fusion.196
  984.2 2.0 copy.137
  992.7 5.9 fusion.90
  998.7 14.0 %scatter_fusion = f32[2,16,1024]{2,0,1:T(2,128)S(1)} fusion(f32[2,16,1024]{2,0,1:T(2,128)S(1)} %split.16, s32[136]{0:T(256)S(1)} %copy-done.16, f32[136,2,1024]{2,1,0:T(2,128)} %get-tuple-element.1103), kind=kCustom, calls=%fused_computation.4 | custom fusion | flops 278528 | bytes 3342880 | tf_op jit(solution)/shard_map/transpose(jvp())/scatter-add | solution.py:39
  1012.7 7.6 scatter_fusion.1
  1021.8 7.6 scatter_fusion.3
  1029.4 7.6 scatter_fusion.2
  1038.3 3.0 pad_maximum_fusion
  1044.8 40.8 %all_to_all.51 = f32[8,128,320]{1,2,0:T(8,128)S(1)} all-to-all(f32[8,128,320]{1,2,0:T(8,128)S(1)} %copy.143), channel_id=1, replica_groups=mesh['seq'=64,'head'=8] {'head'}, dimensions={0} | all-to-all | bytes 2621440 | tf_op jit(solution)/shard_map/all_to_all | solution.py:240
  1085.7 2.1 multiply_reduce_fusion.2
  1090.2 22.5 %psum.14 = f32[3,2560]{1,0:T(4,128)S(1)} all-reduce(f32[3,2560]{1,0:T(4,128)S(1)} %pad_maximum_fusion.5), channel_id=1, replica_groups=mesh['seq'=64,'head'=8] {'head'}, use_global_device_ids=true, to_apply=%region_22.23 | all-reduce | flops 7680 | bytes 61440 | tf_op jit(solution)/shard_map/psum | solution.py:247
  1112.7 248.2 %psum.15 = f32[3,2560]{1,0:T(4,128)} all-reduce(f32[3,2560]{1,0:T(4,128)S(1)} %psum.14), channel_id=1, replica_groups=mesh['seq'=64,'head'=8] {'seq'}, use_global_device_ids=true, to_apply=%region_23.24 | all-reduce | flops 7680 | bytes 61440 | tf_op jit(solution)/shard_map/psum | solution.py:247
  1362.5 4.3 fusion.77
  (789 shorter events, 570.6 us)
Async XLA Ops:
  8.1 8.5 collective-permute-start
  16.6 3.5 copy-start.3
  17.0 3.1 copy-start.5
  20.1 6.9 copy-start.17
  20.1 6.9 copy-start.16
  20.1 40.9 %all-to-all-start = ((f32[128,8,320]{0,2,1:T(8,128)}), f32[128,8,320]{0,2,1:T(8,128)S(1)}, u32[]{:S(2)}, u32[]{:S(2)}) async-start(f32[128,8,320]{0,2,1:T(8,128)} %bitcast.265), calls=%async_computation | async-start | bytes 2621440 | tf_op jit(solution)/shard_map/all_to_all | solution.py:235
  26.2 261.4 %all-gather.9.cloned.1.call-start = ((), (), s32[]{:S(2)}) async-start(), calls=%async_computation.3 | async-start | bytes 10649600 | tf_op jit(solution)/shard_map/all_gather | solution.py:15
  26.3 66.4 %copy-start.15 = (s32[1026]{0:T(1024)}, s32[1026]{0:T(1024)S(1)}, u32[]{:S(2)}) copy-start(s32[1026]{0:T(1024)S(1)} %select_reduce_fusion) | copy-start | bytes 12316
  73.9 3.1 copy-start.18
  84.7 2.3 copy-start.14
  88.4 138.1 %all-to-all-start.1 = ((f32[128,8,256]{0,2,1:T(8,128)}), f32[128,8,256]{0,2,1:T(8,128)S(1)}, u32[]{:S(2)}, u32[]{:S(2)}) async-start(f32[128,8,256]{0,2,1:T(8,128)} %bitcast.273), calls=%async_computation.1 | async-start | bytes 2097152 | tf_op jit(solution)/shard_map/all_to_all | solution.py:236
  91.9 591.0 %all-gather.11.cloned.1.call-start = ((), (), s32[]{:S(2)}) async-start(), calls=%async_computation.4 | async-start | bytes 10649600 | tf_op jit(solution)/shard_map/all_gather | solution.py:15
  230.5 1.7 copy-start.10
  231.6 1.4 copy-start.9
  475.3 1.2 slice-start.1
  589.0 2.9 copy-start.2
  590.9 1.0 copy-start
  986.2 1.7 copy-start.8
  989.7 3.1 copy-start.7
  991.6 7.0 copy-start.1
  998.6 14.0 %copy-start.13 = (f32[136,2,1024]{2,1,0:T(2,128)S(1)}, f32[136,2,1024]{2,1,0:T(2,128)}, u32[]{:S(2)}) copy-start(f32[136,2,1024]{2,1,0:T(2,128)} %get-tuple-element.1102) | copy-start | bytes 3342340
  1020.3 1.4 copy-start.12
  1021.7 7.6 slice-start
  1021.7 7.6 copy-start.11
  1044.8 40.9 %copy-start.4 = (f32[128,2560]{0,1:T(8,128)S(1)}, f32[128,2560]{0,1:T(8,128)}, u32[]{:S(2)}) copy-start(f32[128,2560]{0,1:T(8,128)} %copy-done.3) | copy-start | bytes 3932164
  1044.8 40.8 %copy-start.6 = (f32[2,2560]{0,1:T(8,128)S(1)}, f32[2,2560]{0,1:T(8,128)}, u32[]{:S(2)}) copy-start(f32[2,2560]{0,1:T(8,128)} %copy-done.5) | copy-start | bytes 61444
  1088.2 272.7 %collective-permute-start.1 = (f32[2,2560]{1,0:T(2,128)S(1)}, f32[2,2560]{1,0:T(2,128)S(1)}, u32[]{:S(2)}, u32[]{:S(2)}) collective-permute-start(f32[2,2560]{1,0:T(2,128)S(1)} %copy.144), channel_id=1, source_target_pairs={{1,0},{2,1},{3,2},{4,3},{5,4},{6,5},{7,6},{8,7},{9,8},{10,9},{11,1... | collective-permute-start | bytes 61448 | tf_op jit(solution)/shard_map/ppermute | solution.py:32
Sparse Core Ops, SparseCore 0:
  87.2 91.7 all-gather.8
  594.3 88.6 all-gather.10
